TPU v7x, 32 devices: a whole 2x2x4 slice. The times are simulated.
32 devices in a mesh: src: 8 (over z, y), vox: 4 (over x, core).
Axes of the slice: x: 2, y: 2, z: 4, core: 2. Of those that a mesh axis runs over, the one named last changes fastest.
Arguments:
- forward_voxel_field: bfloat16 [4096, 4096], P('src', 'vox'), may hold values from -0.09375 to 0.09375
- adjoint_voxel_field: bfloat16 [4096, 4096], P('src', 'vox'), may hold values from -6 to 6
- voxel_input_vector: float32 [4096], P('vox'), may hold values from -6 to 6
- measurement_weight: float32 [4096, 4096], P('src', 'vox'), may hold values from 0.00390625 to 0.0390625
Outputs:
- hess_vector: float32 [4096], P('vox')
All inputs are finite; a program needn't handle non-finite values.
Results may differ from a plain program's by a relative error of at most 0.00056.
Values may be sent and summed in bfloat16 or wider, within the bound.
No kernel may reach another device: no remote copies, remote signals or barrier semaphores. Data moves between devices by JAX's collectives and lax.ppermute only.
A program may use at most 64 MiB of HBM per device.

v0:
```python
import jax
import jax.numpy as jnp
from jax import lax
from jax.sharding import PartitionSpec as P


def per_device(forward_voxel_field, adjoint_voxel_field, voxel_input_vector, measurement_weight):
    scaled = (forward_voxel_field.astype(jnp.float32) * voxel_input_vector[None, :]).astype(
        jnp.bfloat16
    )
    adjoint_all = lax.all_gather(adjoint_voxel_field, "src", axis=0, tiled=True)
    predicted_part = lax.dot_general(
        scaled, adjoint_all, (((1,), (1,)), ((), ())), preferred_element_type=jnp.float32
    )
    pred_share = lax.psum_scatter(predicted_part, "vox", scatter_dimension=1, tiled=True)
    weighted_share = (measurement_weight * pred_share).astype(jnp.bfloat16)
    weighted_signal = lax.all_gather(weighted_share, "vox", axis=1, tiled=True)
    back = jnp.dot(weighted_signal, adjoint_all, preferred_element_type=jnp.float32)
    local_sum = jnp.sum(forward_voxel_field.astype(jnp.float32) * back, axis=0)
    return lax.psum(local_sum, "src")


def solution(mesh):
    placed = (P("src", "vox"), P("src", "vox"), P("vox"), P("src", "vox"))
    return jax.shard_map(
        per_device, mesh=mesh, in_specs=placed, out_specs=P("vox"), check_vma=False
    )
```

profile of v0, /device:TPU:0, one launch (start us, length us, event | category | flops | bytes accessed | tf_op | source)
XLA Modules:
  0.0 294.0 jit_solution(4092530594951713219)
XLA Ops:
  6.5 0.0 all-gather.3.cloned.1.call-start
  6.5 0.7 all-gather.3.cloned.1.call-update
  7.3 0.0 reduce-scatter.2.cloned.1.call-start
  7.3 129.8 %all-gather.3.cloned.1.call-done = bf16[4096,1024]{1,0:T(8,128)(2,1)} async-done(((bf16[512,1024]{1,0:T(8,128)(2,1)}), bf16[4096,1024]{1,0:T(8,128)(2,1)}) %all-gather.3.cloned.1.call-update) | async-done | bytes 8388624 | tf_op jit(solution)/shard_map/all_gather | solution.py:11
  137.2 11.5 %fusion.2 = f32[512,4096]{1,0:T(8,128)} fusion(bf16[4096,1024]{1,0:T(8,128)(2,1)} %all-gather.3.cloned.1.call-done, bf16[512,1024]{1,0:T(8,128)(2,1)} %param.4, f32[1024]{0:T(1024)} %param.6), kind=kOutput, calls=%fused_computation.5 | convolution fusion | flops 4296540160 | bytes 17829888 | tf_op jit(solution)/shard_map/dot_general | solution.py:12
  148.7 0.0 copy-start
  148.7 0.0 reduce-scatter.2.cloned.1.call-update
  148.7 0.0 copy-start.1
  148.7 0.0 all-gather.5.cloned.1.call-start
  148.7 70.0 %reduce-scatter.2.cloned.1.call-done = f32[512,1024]{1,0:T(8,128)} async-done(((f32[512,4096]{1,0:T(8,128)}), f32[512,1024]{1,0:T(8,128)}) %reduce-scatter.2.cloned.1.call-update) | async-done | bytes 2097168 | tf_op jit(solution)/shard_map/reduce_scatter | solution.py:15
  218.7 0.0 copy-done
  218.7 2.9 multiply_convert_fusion
  221.7 0.0 all-gather.5.cloned.1.call-update
  221.7 34.6 %all-gather.5.cloned.1.call-done = bf16[512,4096]{1,0:T(8,128)(2,1)} async-done(((bf16[512,1024]{1,0:T(8,128)(2,1)}), bf16[512,4096]{1,0:T(8,128)(2,1)}) %all-gather.5.cloned.1.call-update) | async-done | bytes 4194320 | tf_op jit(solution)/shard_map/all_gather | solution.py:17
  256.3 0.0 copy-done.1
  256.3 9.2 %fusion.1 = f32[1024]{0:T(1024)S(1)} fusion(bf16[512,1024]{1,0:T(8,128)(2,1)S(1)} %copy-done.1, bf16[512,4096]{1,0:T(8,128)(2,1)} %all-gather.5.cloned.1.call-done, bf16[4096,1024]{1,0:T(8,128)(2,1)} %all-gather.3.cloned.1.call-done), kind=kOutput, calls=%fused_computation.3 | convolution fusion | flops 4296539136 | bytes 13635584 | tf_op jit(solution)/shard_map/dot_general | solution.py:18
  265.5 22.0 %psum.7 = f32[1024]{0:T(1024)} all-reduce(f32[1024]{0:T(1024)S(1)} %fusion.1), channel_id=1, replica_groups=mesh['src'=8,'vox'=4] {'src'}, use_global_device_ids=true, to_apply=%region_2.0 | all-reduce | flops 1024 | bytes 8192 | tf_op jit(solution)/shard_map/psum | solution.py:20
Async XLA Ops:
  6.5 130.6 %all-gather.3.cloned.1.call-start = ((), (), s32[]{:S(2)}) async-start(), calls=%async_computation.1 | async-start | bytes 9437184 | tf_op jit(solution)/shard_map/all_gather | solution.py:11
  7.3 211.5 %reduce-scatter.2.cloned.1.call-start = ((), (), s32[]{:S(2)}) async-start(), calls=%async_computation.2 | async-start | bytes 10485760 | tf_op jit(solution)/shard_map/reduce_scatter | solution.py:15
  148.7 70.1 %copy-start = (f32[512,1024]{1,0:T(8,128)S(1)}, f32[512,1024]{1,0:T(8,128)}, u32[]{:S(2)}) copy-start(f32[512,1024]{1,0:T(8,128)} %param.7) | copy-start | bytes 6291460
  148.7 107.7 %copy-start.1 = (bf16[512,1024]{1,0:T(8,128)(2,1)S(1)}, bf16[512,1024]{1,0:T(8,128)(2,1)}, u32[]{:S(2)}) copy-start(bf16[512,1024]{1,0:T(8,128)(2,1)} %param.4) | copy-start | bytes 3145732
  148.7 107.6 %all-gather.5.cloned.1.call-start = ((), (), s32[]{:S(2)}) async-start(), calls=%async_computation.3 | async-start | bytes 5242880 | tf_op jit(solution)/shard_map/all_gather | solution.py:17
Sparse Core Ops, SparseCore 0:
  9.5 127.6 all-gather.2
  148.8 69.8 reduce-scatter.1
  221.8 34.4 all-gather.4
where the time goes:
time: 294 us
  waiting for transfers between devices  235 us (80%)
  blocking collectives  22 us (7%)
  matrix products  20.7 us (7%)
  between operations  13.1 us (4%)
    all_gather x1, waiting for transfers between devices, per_device(): adjoint_all = lax.all_gather(adjoint_voxel_field, 'src', axis=0, tiled=True)  130 us
    reduce_scatter x1, waiting for transfers between devices, per_device(): lax.psum_scatter(predicted_part, 'vox', scatter_dimension=1, tiled=True)  70 us
    all_gather x1, waiting for transfers between devices, per_device(): weighted_signal = lax.all_gather(weighted_share, 'vox', axis=1, tiled=True)  34.6 us
    psum x1, blocking collectives, per_device(): return lax.psum(local_sum, 'src')  22 us
    dot_general x1, matrix products, per_device(): lax.dot_general(scaled, adjoint_all, (((1,), (1,)), ((), ())), preferred_...  11.5 us
    dot_general x1, matrix products, per_device(): jnp.dot(weighted_signal, adjoint_all, preferred_element_type=jnp.float32)  9.15 us
  transfers between devices with their start and end apart: 3, of which 3 were waited for; matrix products, arithmetic and copies ran while one was open for 0% of the time, Pallas kernels for 0%

commit v1 on v0

--- a/solution.py
+++ b/solution.py
@@ -2,6 +2,9 @@
 import jax.numpy as jnp
 from jax import lax
 from jax.sharding import PartitionSpec as P
+from jax.lax import all_gather
+
+render_rates = lambda matrix, mesh_dim: jnp.sum(all_gather(matrix, mesh_dim), axis=0)
 
 
 def per_device(forward_voxel_field, adjoint_voxel_field, voxel_input_vector, measurement_weight):
@@ -17,7 +20,7 @@
     weighted_signal = lax.all_gather(weighted_share, "vox", axis=1, tiled=True)
     back = jnp.dot(weighted_signal, adjoint_all, preferred_element_type=jnp.float32)
     local_sum = jnp.sum(forward_voxel_field.astype(jnp.float32) * back, axis=0)
-    return lax.psum(local_sum, "src")
+    return render_rates(local_sum, "src")
 
 
 def solution(mesh):

time: 294 us -> 303 us (1.031)
  blocking collectives: 22 us -> 30.5 us
    all_gather x0 -> x1, blocking collectives: none -> 30.5 us  [all_gather(matrix, mesh_dim)]
    psum x1 -> x0, blocking collectives: 22 us -> none  [per_device(): return lax.psum(local_sum, 'src')]
where the time goes in v1:
time: 303 us
  waiting for transfers between devices  235 us (78%)
  blocking collectives  30.5 us (10%)
  matrix products  20.7 us (7%)
  between operations  13.1 us (4%)
  other arithmetic  3.53 us (1%)
    all_gather x1, waiting for transfers between devices, per_device(): adjoint_all = lax.all_gather(adjoint_voxel_field, 'src', axis=0, tiled=True)  130 us
    reduce_scatter x1, waiting for transfers between devices, per_device(): lax.psum_scatter(predicted_part, 'vox', scatter_dimension=1, tiled=True)  70 us
    all_gather x1, waiting for transfers between devices, per_device(): weighted_signal = lax.all_gather(weighted_share, 'vox', axis=1, tiled=True)  34.6 us
    all_gather x1, blocking collectives, all_gather(matrix, mesh_dim)  30.5 us
    dot_general x1, matrix products, per_device(): lax.dot_general(scaled, adjoint_all, (((1,), (1,)), ((), ())), preferred_...  11.5 us
    dot_general x1, matrix products, per_device(): jnp.dot(weighted_signal, adjoint_all, preferred_element_type=jnp.float32)  9.15 us
  transfers between devices with their start and end apart: 3, of which 3 were waited for; matrix products, arithmetic and copies ran while one was open for 0% of the time, Pallas kernels for 0%

profile of v1, /device:TPU:0, one launch (start us, length us, event | category | flops | bytes accessed | tf_op | source)
XLA Modules:
  0.0 303.1 jit_solution(7315946149161899780)
XLA Ops:
  6.5 0.0 all-gather.4.cloned.1.call-start
  6.5 0.7 all-gather.4.cloned.1.call-update
  7.3 0.0 reduce-scatter.2.cloned.1.call-start
  7.3 129.8 %all-gather.4.cloned.1.call-done = bf16[4096,1024]{1,0:T(8,128)(2,1)} async-done(((bf16[512,1024]{1,0:T(8,128)(2,1)}), bf16[4096,1024]{1,0:T(8,128)(2,1)}) %all-gather.4.cloned.1.call-update) | async-done | bytes 8388624 | tf_op jit(solution)/shard_map/all_gather | solution.py:14
  137.2 11.5 %fusion.2 = f32[512,4096]{1,0:T(8,128)} fusion(bf16[4096,1024]{1,0:T(8,128)(2,1)} %all-gather.4.cloned.1.call-done, bf16[512,1024]{1,0:T(8,128)(2,1)} %param.4, f32[1024]{0:T(1024)} %param.6), kind=kOutput, calls=%fused_computation.5 | convolution fusion | flops 4296540160 | bytes 17829888 | tf_op jit(solution)/shard_map/dot_general | solution.py:15
  148.7 0.0 copy-start
  148.7 0.0 reduce-scatter.2.cloned.1.call-update
  148.7 0.0 copy-start.1
  148.7 0.0 all-gather.6.cloned.1.call-start
  148.7 70.0 %reduce-scatter.2.cloned.1.call-done = f32[512,1024]{1,0:T(8,128)} async-done(((f32[512,4096]{1,0:T(8,128)}), f32[512,1024]{1,0:T(8,128)}) %reduce-scatter.2.cloned.1.call-update) | async-done | bytes 2097168 | tf_op jit(solution)/shard_map/reduce_scatter | solution.py:18
  218.7 0.0 copy-done
  218.7 2.9 multiply_convert_fusion
  221.7 0.0 all-gather.6.cloned.1.call-update
  221.7 34.6 %all-gather.6.cloned.1.call-done = bf16[512,4096]{1,0:T(8,128)(2,1)} async-done(((bf16[512,1024]{1,0:T(8,128)(2,1)}), bf16[512,4096]{1,0:T(8,128)(2,1)}) %all-gather.6.cloned.1.call-update) | async-done | bytes 4194320 | tf_op jit(solution)/shard_map/all_gather | solution.py:20
  256.3 0.0 copy-done.1
  256.3 9.2 %fusion.1 = f32[1024]{0:T(1024)S(1)} fusion(bf16[512,1024]{1,0:T(8,128)(2,1)S(1)} %copy-done.1, bf16[512,4096]{1,0:T(8,128)(2,1)} %all-gather.6.cloned.1.call-done, bf16[4096,1024]{1,0:T(8,128)(2,1)} %all-gather.4.cloned.1.call-done), kind=kOutput, calls=%fused_computation.3 | convolution fusion | flops 4296539136 | bytes 13635584 | tf_op jit(solution)/shard_map/dot_general | solution.py:21
  265.5 30.5 %all-gather = f32[8192]{0:T(1024)S(1)} all-gather(f32[1024]{0:T(1024)S(1)} %fusion.1), channel_id=2, replica_groups=mesh['src'=8,'vox'=4] {'src'}, dimensions={0}, use_global_device_ids=true | all-gather | bytes 36864 | tf_op jit(solution)/shard_map/all_gather | solution.py:7
  296.0 0.6 reduce_sum.19
  (1 shorter events, 0.0 us)
Async XLA Ops:
  6.5 130.6 %all-gather.4.cloned.1.call-start = ((), (), s32[]{:S(2)}) async-start(), calls=%async_computation.1 | async-start | bytes 9437184 | tf_op jit(solution)/shard_map/all_gather | solution.py:14
  7.3 211.5 %reduce-scatter.2.cloned.1.call-start = ((), (), s32[]{:S(2)}) async-start(), calls=%async_computation.2 | async-start | bytes 10485760 | tf_op jit(solution)/shard_map/reduce_scatter | solution.py:18
  148.7 70.1 %copy-start = (f32[512,1024]{1,0:T(8,128)S(1)}, f32[512,1024]{1,0:T(8,128)}, u32[]{:S(2)}) copy-start(f32[512,1024]{1,0:T(8,128)} %param.7) | copy-start | bytes 6291460
  148.7 107.7 %copy-start.1 = (bf16[512,1024]{1,0:T(8,128)(2,1)S(1)}, bf16[512,1024]{1,0:T(8,128)(2,1)}, u32[]{:S(2)}) copy-start(bf16[512,1024]{1,0:T(8,128)(2,1)} %param.4) | copy-start | bytes 3145732
  148.7 107.6 %all-gather.6.cloned.1.call-start = ((), (), s32[]{:S(2)}) async-start(), calls=%async_computation.3 | async-start | bytes 5242880 | tf_op jit(solution)/shard_map/all_gather | solution.py:20
Sparse Core Ops, SparseCore 0:
  9.5 127.6 all-gather.3
  148.8 69.8 reduce-scatter.1
  221.8 34.4 all-gather.5
